TPU v7x, 256 devices: a whole 4x4x8 slice. The times are simulated.
256 devices in a mesh: rows: 16 (over x, y), sub: 16 (over z, core).
Axes of the slice: x: 4, y: 4, z: 8, core: 2. Of those that a mesh axis runs over, the one named last changes fastest.
Arguments:
- embeddings: bfloat16 [65536, 1024], P(('rows', 'sub'))
- codes: int32 [64, 65536], P(None, ('rows', 'sub')), may hold values from 0 to 255
- codebook: bfloat16 [256, 1024], P(None, 'sub'), may hold values from -6 to 6
Outputs:
- rotation: float32 [1024, 1024], P('sub')
- rotated: bfloat16 [65536, 1024], P(('rows', 'sub'))
- new_codebook: float32 [256, 1024], P(None, 'sub')
All inputs are finite; a program needn't handle non-finite values.
Results may differ from a plain program's by a relative error of at most 0.0095.
Values may be sent and summed in bfloat16 or wider, within the bound.
No kernel may reach another device: no remote copies, remote signals or barrier semaphores. Data moves between devices by JAX's collectives and lax.ppermute only.
A program may use at most 64 MiB of HBM per device.

v0:
```python
import math
import jax
import jax.numpy as jnp
from jax import lax
from jax.sharding import PartitionSpec as P

NS_STEPS = 3
coef_a = 3.4445
coef_b = -4.775
coef_c = 2.0315
frob_eps = 1e-07
highest = lax.Precision.HIGHEST


def rows_dot(left, right):
    return lax.dot_general(
        left, right, (((1,), (1,)), ((), ())), precision=highest, preferred_element_type=jnp.float32
    )


def one_hot_codes(code_block, count_codes):
    levels = lax.broadcasted_iota(jnp.int32, code_block.shape + (count_codes,), 2)
    return (code_block[:, :, None] == levels).astype(jnp.bfloat16)


def decode_rows(codes, table):
    subspaces, local_rows = codes.shape
    count_codes, row_width = table.shape
    sub_width = row_width // subspaces
    block_rows = math.gcd(local_rows, 32768 // subspaces)
    blocks = local_rows // block_rows
    codewords = table.reshape(count_codes, subspaces, sub_width)
    code_blocks = codes.reshape(subspaces, blocks, block_rows).transpose(1, 0, 2)

    def decode_block(unused, code_block):
        one_hot = one_hot_codes(code_block, count_codes)
        picked = jnp.einsum("mnk,kmj->nmj", one_hot, codewords, preferred_element_type=jnp.float32)
        return (unused, picked.reshape(block_rows, row_width).astype(jnp.bfloat16))

    unused, decoded = lax.scan(decode_block, jnp.zeros((), jnp.float32), code_blocks)
    return decoded.reshape(local_rows, row_width)


def codeword_totals(codes, row_values, count_codes):
    subspaces, total_rows = codes.shape
    row_width = row_values.shape[1]
    sub_width = row_width // subspaces
    block_rows = math.gcd(total_rows, 32768 // subspaces)
    blocks = total_rows // block_rows
    code_blocks = codes.reshape(subspaces, blocks, block_rows).transpose(1, 0, 2)
    row_blocks = row_values.reshape(blocks, block_rows, subspaces, sub_width)

    def accumulate(running, pieces):
        one_hot = one_hot_codes(pieces[0], count_codes)
        block_sums = jnp.einsum(
            "mnk,nmj->kmj", one_hot, pieces[1], preferred_element_type=jnp.float32
        )
        block_counts = jnp.sum(one_hot, axis=1, dtype=jnp.float32).T
        return ((running[0] + block_sums, running[1] + block_counts), None)

    initial = (
        jnp.zeros((count_codes, subspaces, sub_width), jnp.float32),
        jnp.zeros((count_codes, subspaces), jnp.float32),
    )
    (code_sums, counts), unused = lax.scan(accumulate, initial, (code_blocks, row_blocks))
    return (code_sums.reshape(count_codes, row_width), counts)


def newton_panel(panel, whole):
    gram_rows = rows_dot(panel, whole)
    quartic = rows_dot(
        jnp.dot(gram_rows, whole, precision=highest, preferred_element_type=jnp.float32), whole
    )
    mixer = coef_b * gram_rows + coef_c * quartic
    return coef_a * panel + jnp.dot(
        mixer, whole, precision=highest, preferred_element_type=jnp.float32
    )


def collect(panel):
    return lax.all_gather(panel, "sub", axis=0, tiled=True)


def body(embeddings, codes, codebook):
    table = lax.all_gather(codebook, "sub", axis=1, tiled=True)
    decoded = decode_rows(codes, table)
    partial_panel = lax.psum_scatter(
        lax.dot_general(
            embeddings, decoded, (((0,), (0,)), ((), ())), preferred_element_type=jnp.float32
        ),
        "sub",
        scatter_dimension=0,
        tiled=True,
    )
    cross_panel = lax.psum(partial_panel, "rows")
    squares = lax.psum(jnp.sum(cross_panel * cross_panel), "sub")
    frob_scale = jnp.sqrt(squares) + frob_eps
    panel = cross_panel / frob_scale
    whole = collect(panel)
    for newton_step in range(NS_STEPS):
        if newton_step > 0:
            whole = collect(panel)
        panel = newton_panel(panel, whole)
    rotation_full = lax.all_gather(panel.astype(jnp.bfloat16), "sub", axis=0, tiled=True)
    rotated = jnp.dot(embeddings, rotation_full, preferred_element_type=jnp.float32).astype(
        jnp.bfloat16
    )
    moved_rows = lax.all_to_all(rotated, "sub", split_axis=1, concat_axis=0, tiled=True)
    moved_codes = lax.all_to_all(codes, "sub", split_axis=0, concat_axis=1, tiled=True)
    code_sums, counts = codeword_totals(moved_codes, moved_rows, table.shape[0])
    code_sums, counts = (
        lax.psum(code_sums.astype(jnp.bfloat16), "rows").astype(jnp.float32),
        lax.psum(counts.astype(jnp.bfloat16), "rows").astype(jnp.float32),
    )
    own_codebook = codebook.astype(jnp.float32)
    spread = jnp.repeat(counts, own_codebook.shape[1] // counts.shape[1], axis=1)
    new_codebook = (code_sums + own_codebook) / (spread + 1.0)
    return (panel, rotated, new_codebook)


def solution(mesh):
    in_specs = (P(("rows", "sub"), None), P(None, ("rows", "sub")), P(None, "sub"))
    out_specs = (P("sub", None), P(("rows", "sub"), None), P(None, "sub"))
    return jax.shard_map(body, mesh=mesh, in_specs=in_specs, out_specs=out_specs, check_vma=False)
```

profile of v0, /device:TPU:64, one launch (start us, length us, event | category | flops | bytes accessed | tf_op | source)
XLA Modules:
  0.0 547.7 jit_solution(3402713358330620616)
XLA Ops:
  7.2 18.8 %all_gather.15 = bf16[256,1024]{0,1:T(8,128)(2,1)S(1)} all-gather(bf16[256,64]{0,1:T(8,128)(2,1)} %param.5), channel_id=1, replica_groups=mesh['rows'=16,'sub'=16] {'sub'}, dimensions={1}, use_global_device_ids=true | all-gather | bytes 557056 | tf_op jit(solution)/shard_map/all_gather | solution.py:85
  26.0 5.3 fusion.6
  31.3 2.7 convolution_bitcast_fusion
  34.0 5.4 copy.15
  39.4 58.3 %reduce-scatter.4.cloned.1.call-done = f32[64,1024]{1,0:T(8,128)} async-done(((f32[1024,1024]{1,0:T(8,128)}), f32[64,1024]{1,0:T(8,128)}) %reduce-scatter.4.cloned.1.call-update) | async-done | bytes 262160 | tf_op jit(solution)/shard_map/reduce_scatter | solution.py:87
  97.8 102.1 %all-reduce.3.cloned.1.call-done = f32[64,1024]{1,0:T(8,128)} async-done(((f32[64,1024]{1,0:T(8,128)}), f32[64,1024]{1,0:T(8,128)}) %all-reduce.3.cloned.1.call-update) | async-done | bytes 262160 | tf_op jit(solution)/shard_map/psum | solution.py:95
  201.5 21.1 %psum.29 = f32[]{:T(128)} all-reduce(f32[]{:T(128)} %multiply_reduce_fusion), channel_id=1, replica_groups=mesh['rows'=16,'sub'=16] {'sub'}, use_global_device_ids=true, to_apply=%region_3.4 | all-reduce | flops 1 | bytes 8 | tf_op jit(solution)/shard_map/psum | solution.py:96
  223.3 1.7 broadcast_divide_fusion
  225.0 43.2 %all-gather.5.cloned.1.call-done = f32[1024,1024]{1,0:T(8,128)} async-done(((f32[64,1024]{1,0:T(8,128)}), f32[1024,1024]{1,0:T(8,128)}) %all-gather.5.cloned.1.call-update) | async-done | bytes 4194320 | tf_op jit(solution)/shard_map/all_gather | solution.py:81
  268.2 6.5 %fusion.12 = f32[64,1024]{1,0:T(8,128)S(1)} fusion(f32[64,1024]{1,0:T(8,128)} %broadcast_divide_fusion, f32[1024,1024]{1,0:T(8,128)} %all-gather.5.cloned.1.call-done), kind=kOutput, calls=%fused_computation.26 | convolution fusion | flops 805306368 | bytes 4718592 | tf_op jit(solution)/shard_map/dot_general | solution.py:16
  274.8 2.6 fusion.13
  277.4 4.2 fusion.9
  281.6 3.4 convolution_add_fusion.2
  285.5 40.1 %all-gather.7.cloned.1.call-done = f32[1024,1024]{1,0:T(8,128)} async-done(((f32[64,1024]{1,0:T(8,128)}), f32[1024,1024]{1,0:T(8,128)}) %all-gather.7.cloned.1.call-update) | async-done | bytes 4194320 | tf_op jit(solution)/shard_map/all_gather | solution.py:81
  325.5 6.5 %fusion.14 = f32[64,1024]{1,0:T(8,128)S(1)} fusion(f32[64,1024]{1,0:T(8,128)} %convolution_add_fusion.2, f32[1024,1024]{1,0:T(8,128)} %all-gather.7.cloned.1.call-done), kind=kOutput, calls=%fused_computation.28 | convolution fusion | flops 805306368 | bytes 4718592 | tf_op jit(solution)/shard_map/dot_general | solution.py:16
  332.0 2.6 fusion.15
  334.7 4.2 fusion.8
  338.9 3.4 convolution_add_fusion.1
  342.5 40.4 %all-gather.9.cloned.1.call-done = f32[1024,1024]{1,0:T(8,128)} async-done(((f32[64,1024]{1,0:T(8,128)}), f32[1024,1024]{1,0:T(8,128)}) %all-gather.9.cloned.1.call-update) | async-done | bytes 4194320 | tf_op jit(solution)/shard_map/all_gather | solution.py:81
  382.8 6.5 %fusion.16 = f32[64,1024]{1,0:T(8,128)S(1)} fusion(f32[64,1024]{1,0:T(8,128)} %convolution_add_fusion.1, f32[1024,1024]{1,0:T(8,128)} %all-gather.9.cloned.1.call-done), kind=kOutput, calls=%fused_computation.30 | convolution fusion | flops 805306368 | bytes 4718592 | tf_op jit(solution)/shard_map/dot_general | solution.py:16
  389.3 2.7 fusion.17
  392.0 4.2 fusion.7
  396.2 3.4 fusion.11
  400.3 6.0 %all-to-all-start.1 = ((s32[16,4,256]{2,1,0:T(4,128)}), s32[16,4,256]{2,1,0:T(4,128)S(1)}, u32[]{:S(2)}, u32[]{:S(2)}) async-start(s32[16,4,256]{2,1,0:T(4,128)} %all_to_all.27), calls=%async_computation.1 | async-start | bytes 131072 | tf_op jit(solution)/shard_map/all_to_all | solution.py:109
  406.3 31.3 %all-gather.11.cloned.1.call-done = bf16[1024,1024]{1,0:T(8,128)(2,1)} async-done(((bf16[64,1024]{1,0:T(8,128)(2,1)}), bf16[1024,1024]{1,0:T(8,128)(2,1)}) %all-gather.11.cloned.1.call-update) | async-done | bytes 2097168 | tf_op jit(solution)/shard_map/all_gather | solution.py:104
  437.6 3.2 convolution_convert_fusion
  440.8 6.4 %all-to-all-start = ((bf16[256,16,64]{0,2,1:T(8,128)(2,1)}), bf16[256,16,64]{0,2,1:T(8,128)(2,1)S(1)}, u32[]{:S(2)}, u32[]{:S(2)}) async-start(bf16[256,16,64]{0,2,1:T(8,128)(2,1)} %bitcast.5), calls=%async_computation | async-start | bytes 1048576 | tf_op jit(solution)/shard_map/all_to_all | solution.py:108
  447.1 6.9 %fusion.3 = bf16[4,256]{1,0:T(4,128)(2,1)S(1)} fusion(s32[4,4096]{1,0:T(4,128)S(1)} %bitcast.55), kind=kLoop, calls=%fused_computation.5 | loop fusion | flops 12581888 | bytes 67584 | tf_op jit(solution)/shard_map/while/body/eval_jaxpr/reduce_sum | solution.py:58
  454.1 2.0 copy.14
  456.1 5.9 %all-to-all-done = bf16[256,16,64]{0,2,1:T(8,128)(2,1)S(1)} async-done(((bf16[256,16,64]{0,2,1:T(8,128)(2,1)}), bf16[256,16,64]{0,2,1:T(8,128)(2,1)S(1)}, u32[]{:S(2)}, u32[]{:S(2)}) %all-to-all-start) | async-done | bytes 524320 | tf_op jit(solution)/shard_map/all_to_all | solution.py:108
  462.5 3.2 fusion.10
  465.8 74.2 %all-reduce = (bf16[256,64]{0,1:T(8,128)(2,1)S(1)}, bf16[256,4]{0,1:T(4,128)(2,1)S(1)}) all-reduce(bf16[256,64]{0,1:T(8,128)(2,1)S(1)} %bitcast.57, bf16[256,4]{0,1:T(4,128)(2,1)S(1)} %bitcast.58), channel_id=1, replica_groups=mesh['rows'=16,'sub'=16] {'rows'}, use_global_device_ids=true, to_apply=%region_4.5 | all-reduce | flops 17408 | bytes 69632 | tf_op jit(solution)/shard_map/psum | solution.py:112
  (37 shorter events, 4.5 us)
Async XLA Ops:
  7.2 24.1 %copy-start = (bf16[256,1024]{1,0:T(8,128)(2,1)S(1)}, bf16[256,1024]{1,0:T(8,128)(2,1)}, u32[]{:S(2)}) copy-start(bf16[256,1024]{1,0:T(8,128)(2,1)} %param.3) | copy-start | bytes 1572868
  7.2 90.5 %reduce-scatter.4.cloned.1.call-start = ((), (), s32[]{:S(2)}) async-start(), calls=%async_computation.8 | async-start | bytes 4456448 | tf_op jit(solution)/shard_map/reduce_scatter | solution.py:87
  39.4 160.5 %all-reduce.3.cloned.1.call-start = ((), (), s32[]{:S(2)}) async-start(), calls=%async_computation.3 | async-start | bytes 524288 | tf_op jit(solution)/shard_map/psum | solution.py:95
  97.7 170.5 %all-gather.5.cloned.1.call-start = ((), (), s32[]{:S(2)}) async-start(), calls=%async_computation.4 | async-start | bytes 4456448 | tf_op jit(solution)/shard_map/all_gather | solution.py:81
  225.0 100.6 %all-gather.7.cloned.1.call-start = ((), (), s32[]{:S(2)}) async-start(), calls=%async_computation.5 | async-start | bytes 4456448 | tf_op jit(solution)/shard_map/all_gather | solution.py:81
  268.2 6.5 %copy-start.2 = (f32[1024,1024]{1,0:T(8,128)S(1)}, f32[1024,1024]{1,0:T(8,128)}, u32[]{:S(2)}) copy-start(f32[1024,1024]{1,0:T(8,128)} %all-gather.5.cloned.1.call-done) | copy-start | bytes 12582916
  274.7 6.8 %copy-start.6 = (f32[64,1024]{1,0:T(8,128)S(1)}, f32[64,1024]{1,0:T(8,128)}, u32[]{:S(2)}) copy-start(f32[64,1024]{1,0:T(8,128)} %broadcast_divide_fusion) | copy-start | bytes 786436
  285.0 97.9 %all-gather.9.cloned.1.call-start = ((), (), s32[]{:S(2)}) async-start(), calls=%async_computation.6 | async-start | bytes 4456448 | tf_op jit(solution)/shard_map/all_gather | solution.py:81
  325.5 6.5 %copy-start.3 = (f32[1024,1024]{1,0:T(8,128)S(1)}, f32[1024,1024]{1,0:T(8,128)}, u32[]{:S(2)}) copy-start(f32[1024,1024]{1,0:T(8,128)} %all-gather.7.cloned.1.call-done) | copy-start | bytes 12582916
  332.0 6.8 %copy-start.5 = (f32[64,1024]{1,0:T(8,128)S(1)}, f32[64,1024]{1,0:T(8,128)}, u32[]{:S(2)}) copy-start(f32[64,1024]{1,0:T(8,128)} %convolution_add_fusion.2) | copy-start | bytes 786436
  342.2 95.4 %all-gather.11.cloned.1.call-start = ((), (), s32[]{:S(2)}) async-start(), calls=%async_computation.7 | async-start | bytes 2228224 | tf_op jit(solution)/shard_map/all_gather | solution.py:104
  382.8 6.5 %copy-start.1 = (f32[1024,1024]{1,0:T(8,128)S(1)}, f32[1024,1024]{1,0:T(8,128)}, u32[]{:S(2)}) copy-start(f32[1024,1024]{1,0:T(8,128)} %all-gather.9.cloned.1.call-done) | copy-start | bytes 12582916
  389.3 6.9 %copy-start.4 = (f32[64,1024]{1,0:T(8,128)S(1)}, f32[64,1024]{1,0:T(8,128)}, u32[]{:S(2)}) copy-start(f32[64,1024]{1,0:T(8,128)} %convolution_add_fusion.1) | copy-start | bytes 786436
  392.0 7.6 %copy-start.8 = (s32[64,256]{1,0:T(8,128)S(1)}, s32[64,256]{1,0:T(8,128)}, u32[]{:S(2)}) copy-start(s32[64,256]{1,0:T(8,128)} %param.4) | copy-start | bytes 196612
  400.3 40.5 %all-to-all-start.1 = ((s32[16,4,256]{2,1,0:T(4,128)}), s32[16,4,256]{2,1,0:T(4,128)S(1)}, u32[]{:S(2)}, u32[]{:S(2)}) async-start(s32[16,4,256]{2,1,0:T(4,128)} %all_to_all.27), calls=%async_computation.1 | async-start | bytes 131072 | tf_op jit(solution)/shard_map/all_to_all | solution.py:109
  440.8 21.2 %all-to-all-start = ((bf16[256,16,64]{0,2,1:T(8,128)(2,1)}), bf16[256,16,64]{0,2,1:T(8,128)(2,1)S(1)}, u32[]{:S(2)}, u32[]{:S(2)}) async-start(bf16[256,16,64]{0,2,1:T(8,128)(2,1)} %bitcast.5), calls=%async_computation | async-start | bytes 1048576 | tf_op jit(solution)/shard_map/all_to_all | solution.py:108
  456.1 83.9 %copy-start.7 = (bf16[256,64]{0,1:T(8,128)(2,1)S(1)}, bf16[256,64]{0,1:T(8,128)(2,1)}, u32[]{:S(2)}) copy-start(bf16[256,64]{0,1:T(8,128)(2,1)} %param.5) | copy-start | bytes 98308
Sparse Core Ops, SparseCore 0:
  39.5 58.1 reduce-scatter.3
  100.9 98.9 all-reduce.2
  225.1 43.1 all-gather.4
  285.1 40.4 all-gather.6
  342.4 40.4 all-gather.8
  399.7 37.8 all-gather.10
where the time goes:
time: 557 us; the launch traced here: 548 us
  waiting for transfers between devices  321 us (58%)
  blocking collectives  114 us (20%)
  matrix products  64.3 us (12%)
  between operations  15.2 us (3%)
  starting transfers between devices  13.3 us (2%)
  other arithmetic  10.9 us (2%)
  local copies, waits for them, and re-layouts  8.64 us (2%)
    all_gather x3, waiting for transfers between devices, collect(): return lax.all_gather(panel, 'sub', axis=0, tiled=True)  124 us
    psum x1, waiting for transfers between devices, body(): cross_panel = lax.psum(partial_panel, 'rows')  102 us
    psum x1, blocking collectives, body(): lax.psum(code_sums.astype(jnp.bfloat16), 'rows').astype(jnp.float32)  74.2 us
    reduce_scatter x1, waiting for transfers between devices, body(): lax.psum_scatter(lax.dot_general(embeddings, decoded, (((0,), (0,)), ((),...  58.3 us
    dot_general x6, matrix products, rows_dot(): lax.dot_general(left, right, (((1,), (1,)), ((), ())), precision=highest,...  31.9 us
    all_gather x1, waiting for transfers between devices, body(): lax.all_gather(panel.astype(jnp.bfloat16), 'sub', axis=0, tiled=True)  31.3 us
    psum x1, blocking collectives, body(): squares = lax.psum(jnp.sum(cross_panel * cross_panel), 'sub')  21.1 us
    all_gather x1, blocking collectives, body(): table = lax.all_gather(codebook, 'sub', axis=1, tiled=True)  18.8 us
  transfers between devices with their start and end apart: 8, of which 7 were waited for; matrix products, arithmetic and copies ran while one was open for 2% of the time, Pallas kernels for 0%

commit v1 on v0

--- a/solution.py
+++ b/solution.py
@@ -92,7 +92,7 @@
         scatter_dimension=0,
         tiled=True,
     )
-    cross_panel = lax.psum(partial_panel, "rows")
+    cross_panel = jnp.sum(lax.all_gather(partial_panel, axis_name="rows"), 0)
     squares = lax.psum(jnp.sum(cross_panel * cross_panel), "sub")
     frob_scale = jnp.sqrt(squares) + frob_eps
     panel = cross_panel / frob_scale

time: 557 us -> 512 us (0.919); the launches traced: 548 us -> 509 us
  waiting for transfers between devices: 321 us -> 282 us
    psum x1 -> x0, waiting for transfers between devices: 102 us -> none  [body(): cross_panel = lax.psum(partial_panel, 'rows')]
    all_gather x0 -> x1, waiting for transfers between devices: none -> 62.8 us  [body(): cross_panel = jnp.sum(lax.all_gather(partial_panel, axis_name='rows'), 0)]
where the time goes in v1:
time: 512 us; the launch traced here: 509 us
  waiting for transfers between devices  282 us (55%)
  blocking collectives  114 us (22%)
  matrix products  64.3 us (13%)
  between operations  15.2 us (3%)
  starting transfers between devices  13.6 us (3%)
  other arithmetic  11.4 us (2%)
  local copies, waits for them, and re-layouts  8.64 us (2%)
    all_gather x3, waiting for transfers between devices, collect(): return lax.all_gather(panel, 'sub', axis=0, tiled=True)  124 us
    psum x1, blocking collectives, body(): lax.psum(code_sums.astype(jnp.bfloat16), 'rows').astype(jnp.float32)  74.2 us
    all_gather x1, waiting for transfers between devices, body(): cross_panel = jnp.sum(lax.all_gather(partial_panel, axis_name='rows'), 0)  62.8 us
    reduce_scatter x1, waiting for transfers between devices, body(): lax.psum_scatter(lax.dot_general(embeddings, decoded, (((0,), (0,)), ((),...  58.3 us
    dot_general x6, matrix products, rows_dot(): lax.dot_general(left, right, (((1,), (1,)), ((), ())), precision=highest,...  31.9 us
    all_gather x1, waiting for transfers between devices, body(): lax.all_gather(panel.astype(jnp.bfloat16), 'sub', axis=0, tiled=True)  31.3 us
    psum x1, blocking collectives, body(): squares = lax.psum(jnp.sum(cross_panel * cross_panel), 'sub')  21.1 us
    all_gather x1, blocking collectives, body(): table = lax.all_gather(codebook, 'sub', axis=1, tiled=True)  18.8 us
  transfers between devices with their start and end apart: 8, of which 7 were waited for; matrix products, arithmetic and copies ran while one was open for 2% of the time, Pallas kernels for 0%

profile of v1, /device:TPU:64, one launch (start us, length us, event | category | flops | bytes accessed | tf_op | source)
XLA Modules:
  0.0 509.3 jit_solution(17758776921306405221)
XLA Ops:
  7.2 18.8 %all_gather.21 = bf16[256,1024]{0,1:T(8,128)(2,1)S(1)} all-gather(bf16[256,64]{0,1:T(8,128)(2,1)} %param.5), channel_id=1, replica_groups=mesh['rows'=16,'sub'=16] {'sub'}, dimensions={1}, use_global_device_ids=true | all-gather | bytes 557056 | tf_op jit(solution)/shard_map/all_gather | solution.py:85
  26.0 5.3 %fusion.6 = bf16[64,256,16]{1,2,0:T(8,128)(2,1)S(1)} fusion(bf16[256,64,16]{0,2,1:T(8,128)(2,1)S(1)} %bitcast.56, s32[64,256]{1,0:T(8,128)} %param.4), kind=kOutput, calls=%fused_computation.9 | convolution fusion | flops 138674176 | bytes 1114112 | tf_op jit(solution)/shard_map/while/body/eval_jaxpr/mnk,kmj->nmj/dot_general | solution.py:37
  31.3 2.7 convolution_bitcast_fusion
  34.0 5.4 %copy.14 = f32[1024,1024]{1,0:T(8,128)} copy(f32[1024,1024]{0,1:T(8,128)} %convolution_bitcast_fusion) | data formatting | bytes 8388608
  39.4 58.3 %reduce-scatter.4.cloned.1.call-done = f32[64,1024]{1,0:T(8,128)} async-done(((f32[1024,1024]{1,0:T(8,128)}), f32[64,1024]{1,0:T(8,128)}) %reduce-scatter.4.cloned.1.call-update) | async-done | bytes 262160 | tf_op jit(solution)/shard_map/reduce_scatter | solution.py:87
  97.8 62.8 %all-gather.15.cloned.1.call-done = f32[1024,1024]{1,0:T(8,128)} async-done(((f32[64,1024]{1,0:T(8,128)}), f32[1024,1024]{1,0:T(8,128)}) %all-gather.15.cloned.1.call-update) | async-done | bytes 4194320 | tf_op jit(solution)/shard_map/all_gather | solution.py:95
  160.6 2.5 reduce_sum.31
  163.7 21.1 %psum.21 = f32[]{:T(128)} all-reduce(f32[]{:T(128)} %multiply_reduce_fusion), channel_id=1, replica_groups=mesh['rows'=16,'sub'=16] {'sub'}, use_global_device_ids=true, to_apply=%region_3.4 | all-reduce | flops 1 | bytes 8 | tf_op jit(solution)/shard_map/psum | solution.py:96
  186.6 43.2 %all-gather.7.cloned.1.call-done = f32[1024,1024]{1,0:T(8,128)} async-done(((f32[64,1024]{1,0:T(8,128)}), f32[1024,1024]{1,0:T(8,128)}) %all-gather.7.cloned.1.call-update) | async-done | bytes 4194320 | tf_op jit(solution)/shard_map/all_gather | solution.py:81
  229.8 6.5 %fusion.12 = f32[64,1024]{1,0:T(8,128)S(1)} fusion(f32[64,1024]{1,0:T(8,128)} %broadcast_divide_fusion, f32[1024,1024]{1,0:T(8,128)} %all-gather.7.cloned.1.call-done), kind=kOutput, calls=%fused_computation.26 | convolution fusion | flops 805306368 | bytes 4718592 | tf_op jit(solution)/shard_map/dot_general | solution.py:16
  236.3 2.6 fusion.13
  238.9 4.2 fusion.9
  243.1 3.4 convolution_add_fusion.2
  247.1 40.0 %all-gather.9.cloned.1.call-done = f32[1024,1024]{1,0:T(8,128)} async-done(((f32[64,1024]{1,0:T(8,128)}), f32[1024,1024]{1,0:T(8,128)}) %all-gather.9.cloned.1.call-update) | async-done | bytes 4194320 | tf_op jit(solution)/shard_map/all_gather | solution.py:81
  287.1 6.5 %fusion.14 = f32[64,1024]{1,0:T(8,128)S(1)} fusion(f32[64,1024]{1,0:T(8,128)} %convolution_add_fusion.2, f32[1024,1024]{1,0:T(8,128)} %all-gather.9.cloned.1.call-done), kind=kOutput, calls=%fused_computation.28 | convolution fusion | flops 805306368 | bytes 4718592 | tf_op jit(solution)/shard_map/dot_general | solution.py:16
  293.6 2.6 fusion.15
  296.2 4.2 fusion.8
  300.4 3.4 convolution_add_fusion.1
  304.0 40.4 %all-gather.11.cloned.1.call-done = f32[1024,1024]{1,0:T(8,128)} async-done(((f32[64,1024]{1,0:T(8,128)}), f32[1024,1024]{1,0:T(8,128)}) %all-gather.11.cloned.1.call-update) | async-done | bytes 4194320 | tf_op jit(solution)/shard_map/all_gather | solution.py:81
  344.4 6.5 %fusion.16 = f32[64,1024]{1,0:T(8,128)S(1)} fusion(f32[64,1024]{1,0:T(8,128)} %convolution_add_fusion.1, f32[1024,1024]{1,0:T(8,128)} %all-gather.11.cloned.1.call-done), kind=kOutput, calls=%fused_computation.30 | convolution fusion | flops 805306368 | bytes 4718592 | tf_op jit(solution)/shard_map/dot_general | solution.py:16
  350.9 2.7 fusion.17
  353.5 4.2 fusion.7
  357.7 3.4 fusion.11
  361.8 6.0 %all-to-all-start.1 = ((s32[16,4,256]{2,1,0:T(4,128)}), s32[16,4,256]{2,1,0:T(4,128)S(1)}, u32[]{:S(2)}, u32[]{:S(2)}) async-start(s32[16,4,256]{2,1,0:T(4,128)} %all_to_all.27), calls=%async_computation.1 | async-start | bytes 131072 | tf_op jit(solution)/shard_map/all_to_all | solution.py:109
  367.8 31.3 %all-gather.13.cloned.1.call-done = bf16[1024,1024]{1,0:T(8,128)(2,1)} async-done(((bf16[64,1024]{1,0:T(8,128)(2,1)}), bf16[1024,1024]{1,0:T(8,128)(2,1)}) %all-gather.13.cloned.1.call-update) | async-done | bytes 2097168 | tf_op jit(solution)/shard_map/all_gather | solution.py:104
  399.1 3.2 convolution_convert_fusion
  402.3 6.4 %all-to-all-start = ((bf16[256,16,64]{0,2,1:T(8,128)(2,1)}), bf16[256,16,64]{0,2,1:T(8,128)(2,1)S(1)}, u32[]{:S(2)}, u32[]{:S(2)}) async-start(bf16[256,16,64]{0,2,1:T(8,128)(2,1)} %bitcast.6), calls=%async_computation | async-start | bytes 1048576 | tf_op jit(solution)/shard_map/all_to_all | solution.py:108
  408.7 6.9 %fusion.3 = bf16[4,256]{1,0:T(4,128)(2,1)S(1)} fusion(s32[4,4096]{1,0:T(4,128)S(1)} %bitcast.57), kind=kLoop, calls=%fused_computation.5 | loop fusion | flops 12581888 | bytes 67584 | tf_op jit(solution)/shard_map/while/body/eval_jaxpr/reduce_sum | solution.py:58
  415.6 2.0 copy.13
  417.6 5.9 %all-to-all-done = bf16[256,16,64]{0,2,1:T(8,128)(2,1)S(1)} async-done(((bf16[256,16,64]{0,2,1:T(8,128)(2,1)}), bf16[256,16,64]{0,2,1:T(8,128)(2,1)S(1)}, u32[]{:S(2)}, u32[]{:S(2)}) %all-to-all-start) | async-done | bytes 524320 | tf_op jit(solution)/shard_map/all_to_all | solution.py:108
  424.1 3.2 fusion.10
  427.3 74.2 %all-reduce = (bf16[256,64]{0,1:T(8,128)(2,1)S(1)}, bf16[256,4]{0,1:T(4,128)(2,1)S(1)}) all-reduce(bf16[256,64]{0,1:T(8,128)(2,1)S(1)} %bitcast.59, bf16[256,4]{0,1:T(4,128)(2,1)S(1)} %bitcast.60), channel_id=1, replica_groups=mesh['rows'=16,'sub'=16] {'rows'}, use_global_device_ids=true, to_apply=%region_4.5 | all-reduce | flops 17408 | bytes 69632 | tf_op jit(solution)/shard_map/psum | solution.py:112
  (38 shorter events, 4.6 us)
Async XLA Ops:
  7.2 24.1 %copy-start = (bf16[256,1024]{1,0:T(8,128)(2,1)S(1)}, bf16[256,1024]{1,0:T(8,128)(2,1)}, u32[]{:S(2)}) copy-start(bf16[256,1024]{1,0:T(8,128)(2,1)} %param.3) | copy-start | bytes 1572868
  7.2 90.5 %reduce-scatter.4.cloned.1.call-start = ((), (), s32[]{:S(2)}) async-start(), calls=%async_computation.8 | async-start | bytes 4456448 | tf_op jit(solution)/shard_map/reduce_scatter | solution.py:87
  39.4 121.2 %all-gather.15.cloned.1.call-start = ((), (), s32[]{:S(2)}) async-start(), calls=%async_computation.7 | async-start | bytes 4456448 | tf_op jit(solution)/shard_map/all_gather | solution.py:95
  97.7 132.1 %all-gather.7.cloned.1.call-start = ((), (), s32[]{:S(2)}) async-start(), calls=%async_computation.3 | async-start | bytes 4456448 | tf_op jit(solution)/shard_map/all_gather | solution.py:81
  186.3 100.8 %all-gather.9.cloned.1.call-start = ((), (), s32[]{:S(2)}) async-start(), calls=%async_computation.4 | async-start | bytes 4456448 | tf_op jit(solution)/shard_map/all_gather | solution.py:81
  229.8 6.5 %copy-start.2 = (f32[1024,1024]{1,0:T(8,128)S(1)}, f32[1024,1024]{1,0:T(8,128)}, u32[]{:S(2)}) copy-start(f32[1024,1024]{1,0:T(8,128)} %all-gather.7.cloned.1.call-done) | copy-start | bytes 12582916
  236.3 6.8 %copy-start.6 = (f32[64,1024]{1,0:T(8,128)S(1)}, f32[64,1024]{1,0:T(8,128)}, u32[]{:S(2)}) copy-start(f32[64,1024]{1,0:T(8,128)} %broadcast_divide_fusion) | copy-start | bytes 786436
  246.5 97.9 %all-gather.11.cloned.1.call-start = ((), (), s32[]{:S(2)}) async-start(), calls=%async_computation.5 | async-start | bytes 4456448 | tf_op jit(solution)/shard_map/all_gather | solution.py:81
  287.1 6.5 %copy-start.3 = (f32[1024,1024]{1,0:T(8,128)S(1)}, f32[1024,1024]{1,0:T(8,128)}, u32[]{:S(2)}) copy-start(f32[1024,1024]{1,0:T(8,128)} %all-gather.9.cloned.1.call-done) | copy-start | bytes 12582916
  293.6 6.8 %copy-start.5 = (f32[64,1024]{1,0:T(8,128)S(1)}, f32[64,1024]{1,0:T(8,128)}, u32[]{:S(2)}) copy-start(f32[64,1024]{1,0:T(8,128)} %convolution_add_fusion.2) | copy-start | bytes 786436
  303.8 95.4 %all-gather.13.cloned.1.call-start = ((), (), s32[]{:S(2)}) async-start(), calls=%async_computation.6 | async-start | bytes 2228224 | tf_op jit(solution)/shard_map/all_gather | solution.py:104
  344.4 6.5 %copy-start.1 = (f32[1024,1024]{1,0:T(8,128)S(1)}, f32[1024,1024]{1,0:T(8,128)}, u32[]{:S(2)}) copy-start(f32[1024,1024]{1,0:T(8,128)} %all-gather.11.cloned.1.call-done) | copy-start | bytes 12582916
  350.9 6.9 %copy-start.4 = (f32[64,1024]{1,0:T(8,128)S(1)}, f32[64,1024]{1,0:T(8,128)}, u32[]{:S(2)}) copy-start(f32[64,1024]{1,0:T(8,128)} %convolution_add_fusion.1) | copy-start | bytes 786436
  353.5 7.6 %copy-start.8 = (s32[64,256]{1,0:T(8,128)S(1)}, s32[64,256]{1,0:T(8,128)}, u32[]{:S(2)}) copy-start(s32[64,256]{1,0:T(8,128)} %param.4) | copy-start | bytes 196612
  361.8 40.5 %all-to-all-start.1 = ((s32[16,4,256]{2,1,0:T(4,128)}), s32[16,4,256]{2,1,0:T(4,128)S(1)}, u32[]{:S(2)}, u32[]{:S(2)}) async-start(s32[16,4,256]{2,1,0:T(4,128)} %all_to_all.27), calls=%async_computation.1 | async-start | bytes 131072 | tf_op jit(solution)/shard_map/all_to_all | solution.py:109
  402.3 21.2 %all-to-all-start = ((bf16[256,16,64]{0,2,1:T(8,128)(2,1)}), bf16[256,16,64]{0,2,1:T(8,128)(2,1)S(1)}, u32[]{:S(2)}, u32[]{:S(2)}) async-start(bf16[256,16,64]{0,2,1:T(8,128)(2,1)} %bitcast.6), calls=%async_computation | async-start | bytes 1048576 | tf_op jit(solution)/shard_map/all_to_all | solution.py:108
  417.6 83.9 %copy-start.7 = (bf16[256,64]{0,1:T(8,128)(2,1)S(1)}, bf16[256,64]{0,1:T(8,128)(2,1)}, u32[]{:S(2)}) copy-start(bf16[256,64]{0,1:T(8,128)(2,1)} %param.5) | copy-start | bytes 98308
Sparse Core Ops, SparseCore 0:
  39.5 58.1 reduce-scatter.3
  100.1 60.4 all-gather.14
  186.4 43.3 all-gather.6
  246.6 40.4 all-gather.8
  303.9 40.4 all-gather.10
  361.3 37.8 all-gather.12
